TPU v7x, 512 devices: a whole 4x8x8 slice. The times are simulated.
512 devices in a mesh: freq: 16 (over y, core), trace: 32 (over z, x).
Axes of the slice: x: 4, y: 8, z: 8, core: 2. Of those that a mesh axis runs over, the one named last changes fastest.
Arguments:
- traces: bfloat16 [64, 128, 2048], P('trace', 'freq'), may hold values from -20 to 20
- omega: float32 [2, 33, 64, 64], replicated, may hold values from -0.125 to 0.125
Outputs:
- denoised: float32 [64, 128, 2048], P('trace', 'freq')
All inputs are finite; a program needn't handle non-finite values.
Results may differ from a plain program's by a relative error of at most 0.0003.
Values sent between devices are 32-bit elements; how exact they have to be, the bound alone decides.
No kernel may reach another device: no remote copies, remote signals or barrier semaphores. Data moves between devices by JAX's collectives and lax.ppermute only.
A program may use at most 64 MiB of HBM per device.

v0:
```python
import math
import jax
import jax.numpy as jnp
from jax import lax
from jax.sharding import PartitionSpec as P

FREQ_DEV = 1
highest = lax.Precision.HIGHEST


def fourier_tables(samples, freq_total):
    moments = jnp.arange(samples, dtype=jnp.int32)
    bins = jnp.arange(freq_total, dtype=jnp.int32) + 1
    phases = bins[:, None] * moments[None, :] % samples
    angles = phases.astype(jnp.float32) * (2.0 * math.pi / samples)
    return (jnp.cos(angles), jnp.sin(angles))


def anti_counts(spots, length, window, lags):
    counted = jnp.minimum(jnp.minimum(spots + 1, length - spots), min(window, lags))
    return counted.astype(jnp.float32)


def solve_one(factor, right_side):
    return jax.scipy.linalg.cho_solve((factor, True), right_side)


def body(traces, omega):
    rows_dev, cols_dev, samples = traces.shape
    lag_x, lag_y, rank_size = (omega.shape[1], omega.shape[2], omega.shape[3])
    trace_count = lax.axis_size("trace")
    freq_count = lax.axis_size("freq")
    patch_x = rows_dev * trace_count
    patch_y = cols_dev * freq_count
    win_x = patch_x - lag_x + 1
    win_y = patch_y - lag_y + 1
    freq_total = FREQ_DEV * freq_count
    own_rows = win_x // trace_count
    own_lags = lag_y // trace_count
    position = lax.axis_index("trace")
    cosine_table, sine_table = fourier_tables(samples, freq_total)
    norm_scale = 1.0 / math.sqrt(samples)
    forward = jnp.stack([cosine_table.T, -sine_table.T], axis=1) * norm_scale
    spectrum = jnp.einsum("xyt,tpk->xypk", traces.astype(jnp.float32), forward, precision=highest)
    spectrum = lax.all_to_all(spectrum, "freq", split_axis=3, concat_axis=1, tiled=True)
    slices = jnp.transpose(spectrum, (3, 2, 0, 1))
    whole_slices = lax.all_gather(slices, "trace", axis=2, tiled=True)
    freq_dev = whole_slices.shape[0]
    first_row = position * own_rows
    row_slabs = jnp.stack([lax.dynamic_slice_in_dim(whole_slices, first_row + 0, lag_x, 2)], axis=1)
    hankel = jnp.stack([row_slabs[..., anchor : anchor + lag_y] for anchor in range(win_y)], axis=3)
    hankel_flat = hankel.reshape(freq_dev, own_rows * 2 * win_y, lag_x * lag_y)
    omega_flat = omega.reshape(2, lag_x * lag_y, rank_size)
    products = jnp.einsum("fnm,smq->fnsq", hankel_flat, omega_flat, precision=highest)
    products = products.reshape(freq_dev, own_rows, 2, win_y, 2, rank_size)
    sketch_re = products[:, :, 0, :, 0] - products[:, :, 1, :, 1]
    sketch_im = products[:, :, 0, :, 1] + products[:, :, 1, :, 0]
    own_sketch = jnp.transpose(jnp.concatenate([sketch_re, sketch_im], -1), (1, 0, 2, 3))
    sketch = lax.all_gather(own_sketch, "trace", axis=0, tiled=True)
    inner = lax.psum(
        jnp.einsum("afbp,afbq->fpq", own_sketch, own_sketch, precision=highest), "trace"
    )
    lag_start = position * own_lags
    hankel_blocks = []
    for offset in range(own_lags):
        band = lax.dynamic_slice_in_dim(whole_slices, lag_start + offset, win_y, 3)
        hankel_blocks.append(
            jnp.stack([band[:, :, anchor : anchor + win_x] for anchor in range(lag_x)], axis=2)
        )
    columns = jnp.stack(hankel_blocks, axis=1).reshape(
        freq_dev, own_lags * 2 * lag_x, win_x * win_y
    )
    flat_sketch = jnp.transpose(sketch, (1, 0, 2, 3)).reshape(
        freq_dev, win_x * win_y, 2 * rank_size
    )
    project = jnp.einsum("fnm,fmq->fnq", columns, flat_sketch, precision=highest).reshape(
        freq_dev, own_lags, 2, lag_x, 2 * rank_size
    )
    proj_re = jnp.transpose(
        project[:, :, 0, :, :rank_size] + project[:, :, 1, :, rank_size:], (0, 3, 1, 2)
    )
    proj_im = jnp.transpose(
        project[:, :, 1, :, :rank_size] - project[:, :, 0, :, rank_size:], (0, 3, 1, 2)
    )
    gram_re = inner[:, :rank_size, :rank_size] + inner[:, rank_size:, rank_size:]
    gram_im = inner[:, :rank_size, rank_size:] - inner[:, rank_size:, :rank_size]
    real_gram = jnp.concatenate(
        [jnp.concatenate([gram_re, -gram_im], 2), jnp.concatenate([gram_im, gram_re], 2)], 1
    )
    right_side = jnp.concatenate([proj_re, proj_im], 1).reshape(
        freq_dev, 2 * rank_size, own_lags * lag_x
    )
    factor = jnp.linalg.cholesky(real_gram)
    solved = jax.vmap(solve_one)(factor, right_side)
    mix_re = solved[:, :rank_size]
    mix_im = solved[:, rank_size:]
    mix_real = jnp.concatenate([mix_re, -mix_im], 1).reshape(
        freq_dev, 2 * rank_size, own_lags, lag_x
    )
    mix_imag = jnp.concatenate([mix_im, mix_re], 1).reshape(
        freq_dev, 2 * rank_size, own_lags, lag_x
    )
    mixing = jnp.stack([mix_real, mix_imag], axis=3)
    sketch_cols = jnp.transpose(sketch, (1, 2, 3, 0))
    lowrank = jnp.einsum("fqezc,fbqa->fbezca", mixing, sketch_cols, precision=highest)
    target = (
        jnp.arange(lag_x, dtype=jnp.int32)[:, None] + jnp.arange(win_x, dtype=jnp.int32)[None, :]
    ).reshape(-1)
    diagonal = (target[:, None] == jnp.arange(patch_x, dtype=jnp.int32)[None, :]).astype(
        jnp.float32
    )
    spread = jnp.dot(lowrank.reshape(-1, lag_x * win_x), diagonal, precision=highest).reshape(
        freq_dev, win_y, own_lags, 2, patch_x
    )
    partial_value = jnp.zeros((patch_x, freq_dev, 2, patch_y), jnp.float32)
    zero_index = jnp.zeros((), jnp.int32)
    for offset in range(own_lags):
        band_block = jnp.transpose(spread[:, :, offset], (3, 0, 2, 1))
        partial_value = partial_value + lax.dynamic_update_slice(
            jnp.zeros_like(partial_value),
            band_block,
            (zero_index, zero_index, zero_index, lag_start + offset),
        )
    averaged = lax.psum_scatter(partial_value, "trace", scatter_dimension=0, tiled=True)
    spots_x = position * rows_dev + jnp.arange(rows_dev, dtype=jnp.int32)
    spots_y = jnp.arange(patch_y, dtype=jnp.int32)
    counts = (
        anti_counts(spots_x, patch_x, win_x, lag_x)[:, None, None, None]
        * anti_counts(spots_y, patch_y, win_y, lag_y)[None, None, None, :]
    )
    averaged = averaged / counts
    returned = lax.all_to_all(averaged, "freq", split_axis=3, concat_axis=1, tiled=True)
    inverse = jnp.stack([cosine_table, -sine_table], axis=1) * (2.0 * norm_scale)
    return jnp.einsum("xkpy,kpt->xyt", returned, inverse, precision=highest)


def solution(mesh):
    return jax.shard_map(
        body,
        mesh=mesh,
        in_specs=(P("trace", "freq", None), P()),
        out_specs=P("trace", "freq", None),
        check_vma=False,
    )
```

profile of v0, /device:TPU:1, one launch (start us, length us, event | category | flops | bytes accessed | tf_op | source)
XLA Modules:
  0.0 583.4 jit_solution(9340026111584924302)
XLA Ops:
  7.2 1.4 convolution_bitcast_fusion.5
  9.3 10.1 %all-to-all-start = ((f32[2,8,2,16]{1,0,2,3:T(2,128)}), f32[2,8,2,16]{1,0,2,3:T(2,128)S(1)}, u32[]{:S(2)}, u32[]{:S(2)}) async-start(f32[2,8,2,16]{1,0,2,3:T(2,128)} %copy.367), calls=%async_computation | async-start | bytes 65536 | tf_op jit(solution)/shard_map/all_to_all | solution.py:45
  19.5 7.4 %all-to-all-done = f32[2,8,2,16]{1,0,2,3:T(2,128)S(1)} async-done(((f32[2,8,2,16]{1,0,2,3:T(2,128)}), f32[2,8,2,16]{1,0,2,3:T(2,128)S(1)}, u32[]{:S(2)}, u32[]{:S(2)}) %all-to-all-start) | async-done | bytes 2080 | tf_op jit(solution)/shard_map/all_to_all | solution.py:45
  27.0 41.2 %all_gather.6 = f32[1,2,64,128]{3,1,0,2:T(2,128)S(1)} all-gather(f32[1,2,2,128]{3,1,0,2:T(2,128)S(1)} %bitcast.277), channel_id=1, replica_groups=mesh['freq'=16,'trace'=32] {'trace'}, dimensions={2}, use_global_device_ids=true | all-gather | bytes 67584 | tf_op jit(solution)/shard_map/all_gather | solution.py:47
  68.2 1.6 fusion.69
  69.8 1.4 fusion.68
  71.9 1.0 fusion.70
  73.0 0.8 copy.379
  74.4 0.8 copy.380
  75.9 0.8 copy.381
  77.3 0.8 copy.382
  78.8 0.8 copy.383
  80.2 0.8 copy.384
  81.7 0.8 copy.385
  83.1 0.8 copy.386
  84.6 0.8 copy.387
  86.0 0.8 copy.388
  87.5 0.8 copy.389
  88.9 0.8 copy.390
  90.4 0.8 copy.391
  91.8 0.8 copy.392
  93.3 0.8 copy.393
  94.7 0.8 copy.394
  96.2 0.8 copy.395
  97.6 0.8 copy.396
  99.1 0.8 copy.397
  133.9 9.0 %stack.490 = f32[2,65,2112]{2,1,0:T(8,128)S(1)} concatenate(f32[2,1,2112]{2,1,0:T(1,128)} %stack.562, f32[2,1,2112]{2,1,0:T(1,128)} %stack.563, f32[2,1,2112]{2,1,0:T(1,128)} %stack.564, f32[2,1,2112]{2,1,0:T(1,128)} %stack.565, f32[2,1,2112]{2,1,0:T(1,128)} %stack.566, f32[2,1,2112]{2,1,0:T(1,128)} %stack.567, f32[2,1,2112]{2,1,0:T(1,128)} %stack.568, f32[2,1,2112]{2,1,0:T(1,128)} %stack.569, ...), dimensions={1} | concatenate | bytes 2196480 | tf_op jit(solution)/shard_map/stack | solution.py:51
  142.9 3.6 fusion.6
  146.6 0.9 convolution_bitcast_fusion.3
  149.8 1.2 constant_dynamic-slice_fusion.65
  163.3 1.8 constant_dynamic-slice_fusion.47
  199.0 5.5 stack.524
  204.6 6.3 %stack.558 = f32[1,2,33,2080]{3,2,1,0:T(8,128)} concatenate(f32[1,2,1,2080]{3,2,1,0:T(1,128)S(1)} %copy-done.37, f32[1,2,1,2080]{3,2,1,0:T(1,128)} %stack.526, f32[1,2,1,2080]{3,2,1,0:T(1,128)} %stack.527, f32[1,2,1,2080]{3,2,1,0:T(1,128)} %stack.528, f32[1,2,1,2080]{3,2,1,0:T(1,128)S(1)} %copy-done.48, f32[1,2,1,2080]{3,2,1,0:T(1,128)S(1)} %copy-done.49, ...), dimensions={2} | concatenate | bytes 1098240 | tf_op jit(solution)/shard_map/stack | solution.py:68
  211.0 89.0 %all-reduce.4.cloned.1.call-done = f32[1,128,128]{1,2,0:T(8,128)} async-done(((f32[1,128,128]{1,2,0:T(8,128)}), f32[1,128,128]{1,2,0:T(8,128)}) %all-reduce.4.cloned.1.call-update) | async-done | bytes 65552 | tf_op jit(solution)/shard_map/psum | solution.py:60
  299.9 0.9 fusion.66
  301.2 11.9 %custom-call.11 = f32[1,128,128]{2,1,0:T(8,128)S(1)} custom-call(f32[1,128,128]{2,1,0:T(8,128)S(1)} %fusion.46), custom_call_target="Cholesky" | custom-call | tf_op jit(solution)/shard_map/jit(cholesky)/cholesky | solution.py:93
  314.4 9.8 %custom-call.12 = f32[1,1,128,128]{2,3,1,0:T(8,128)S(1)} custom-call(f32[1,1,128,128]{3,2,1,0:T(8,128)S(1)} %fusion.41), custom_call_target="InvertDiagBlocksLowerTriangular" | custom-call | tf_op jit(solution)/shard_map/vmap(jit(_cho_solve))/triangular_solve | solution.py:25
  324.2 58.3 %all-gather.2.cloned.1.call-done = f32[32,1,65,128]{3,1,2,0:T(1,128)} async-done(((f32[1,1,65,128]{3,1,2,0:T(1,128)}), f32[32,1,65,128]{3,1,2,0:T(1,128)}) %all-gather.2.cloned.1.call-update) | async-done | bytes 1064976 | tf_op jit(solution)/shard_map/all_gather | solution.py:59
  382.6 3.1 fusion.9
  386.6 5.1 convolution_bitcast_fusion.1
  391.8 6.0 %copy.575 = f32[1,65,2,2,33,32]{1,5,4,3,2,0:T(8,128)} copy(f32[1,65,2,2,33,32]{4,5,3,2,1,0:T(8,128)} %convolution_bitcast_fusion.1) | data formatting | bytes 2196480 | tf_op jit(solution)/shard_map/fqezc,fbqa->fbezca/transpose | solution.py:105
  397.8 2.6 convolution_bitcast_fusion.2
  402.2 1.3 dynamic-slice.1
  404.1 149.5 %all-reduce.6.cloned.1.call-done = f32[64,1,2,128]{3,0,2,1:T(8,128)} async-done(((f32[64,1,2,128]{3,0,2,1:T(8,128)}), f32[64,1,2,128]{3,0,2,1:T(8,128)}) %all-reduce.6.cloned.1.call-update) | async-done | bytes 65552
  554.3 0.8 copy.577
  555.1 11.8 %all-to-all-start.1 = ((f32[2,1,2,128]{0,2,1,3:T(2,128)}), f32[2,1,2,128]{0,2,1,3:T(2,128)S(1)}, u32[]{:S(2)}, u32[]{:S(2)}) async-start(f32[2,1,2,128]{0,2,1,3:T(2,128)} %copy.577), calls=%async_computation.1 | async-start | bytes 262144 | tf_op jit(solution)/shard_map/all_to_all | solution.py:132
  567.4 8.3 %all-to-all-done.1 = f32[2,1,2,128]{0,2,1,3:T(2,128)S(1)} async-done(((f32[2,1,2,128]{0,2,1,3:T(2,128)}), f32[2,1,2,128]{0,2,1,3:T(2,128)S(1)}, u32[]{:S(2)}, u32[]{:S(2)}) %all-to-all-start.1) | async-done | bytes 2080 | tf_op jit(solution)/shard_map/all_to_all | solution.py:132
  575.9 1.0 convolution_bitcast_fusion
  (402 shorter events, 102.1 us)
Async XLA Ops:
  6.5 136.4 %copy-start = (f32[2,33,64,64]{3,2,1,0:T(8,128)S(1)}, f32[2,33,64,64]{3,2,1,0:T(8,128)}, u32[]{:S(2)}) copy-start(f32[2,33,64,64]{3,2,1,0:T(8,128)} %param.3) | copy-start | bytes 3244036
  9.3 17.6 %all-to-all-start = ((f32[2,8,2,16]{1,0,2,3:T(2,128)}), f32[2,8,2,16]{1,0,2,3:T(2,128)S(1)}, u32[]{:S(2)}, u32[]{:S(2)}) async-start(f32[2,8,2,16]{1,0,2,3:T(2,128)} %copy.367), calls=%async_computation | async-start | bytes 65536 | tf_op jit(solution)/shard_map/all_to_all | solution.py:45
  19.4 280.5 %all-reduce.4.cloned.1.call-start = ((), (), s32[]{:S(2)}) async-start(), calls=%async_computation.3 | async-start | bytes 131072 | tf_op jit(solution)/shard_map/psum | solution.py:60
  113.8 14.5 %copy-start.10 = (f32[1,1,2,33,64]{4,2,3,1,0:T(2,128)S(1)}, f32[1,1,2,33,64]{4,2,3,1,0:T(2,128)}, u32[]{:S(2)}) copy-start(f32[1,1,2,33,64]{4,2,3,1,0:T(2,128)} %get-tuple-element.145) | copy-start | bytes 50692
  114.5 14.5 %copy-start.9 = (f32[1,1,2,33,64]{4,2,3,1,0:T(2,128)S(1)}, f32[1,1,2,33,64]{4,2,3,1,0:T(2,128)}, u32[]{:S(2)}) copy-start(f32[1,1,2,33,64]{4,2,3,1,0:T(2,128)} %get-tuple-element.144) | copy-start | bytes 50692
  115.2 14.6 %copy-start.8 = (f32[1,1,2,33,64]{4,2,3,1,0:T(2,128)S(1)}, f32[1,1,2,33,64]{4,2,3,1,0:T(2,128)}, u32[]{:S(2)}) copy-start(f32[1,1,2,33,64]{4,2,3,1,0:T(2,128)} %get-tuple-element.143) | copy-start | bytes 50692
  115.9 14.5 %copy-start.7 = (f32[1,1,2,33,64]{4,2,3,1,0:T(2,128)S(1)}, f32[1,1,2,33,64]{4,2,3,1,0:T(2,128)}, u32[]{:S(2)}) copy-start(f32[1,1,2,33,64]{4,2,3,1,0:T(2,128)} %get-tuple-element.142) | copy-start | bytes 50692
  116.6 14.5 %copy-start.6 = (f32[1,1,2,33,64]{4,2,3,1,0:T(2,128)S(1)}, f32[1,1,2,33,64]{4,2,3,1,0:T(2,128)}, u32[]{:S(2)}) copy-start(f32[1,1,2,33,64]{4,2,3,1,0:T(2,128)} %get-tuple-element.141) | copy-start | bytes 50692
  117.3 14.5 %copy-start.5 = (f32[1,1,2,33,64]{4,2,3,1,0:T(2,128)S(1)}, f32[1,1,2,33,64]{4,2,3,1,0:T(2,128)}, u32[]{:S(2)}) copy-start(f32[1,1,2,33,64]{4,2,3,1,0:T(2,128)} %get-tuple-element.140) | copy-start | bytes 50692
  118.0 14.6 %copy-start.4 = (f32[1,1,2,33,64]{4,2,3,1,0:T(2,128)S(1)}, f32[1,1,2,33,64]{4,2,3,1,0:T(2,128)}, u32[]{:S(2)}) copy-start(f32[1,1,2,33,64]{4,2,3,1,0:T(2,128)} %get-tuple-element.139) | copy-start | bytes 50692
  118.7 14.5 %copy-start.3 = (f32[1,1,2,33,64]{4,2,3,1,0:T(2,128)S(1)}, f32[1,1,2,33,64]{4,2,3,1,0:T(2,128)}, u32[]{:S(2)}) copy-start(f32[1,1,2,33,64]{4,2,3,1,0:T(2,128)} %get-tuple-element.138) | copy-start | bytes 50692
  119.4 14.6 %copy-start.51 = (f32[2,1,2112]{2,1,0:T(1,128)S(1)}, f32[2,1,2112]{2,1,0:T(1,128)}, u32[]{:S(2)}) copy-start(f32[2,1,2112]{2,1,0:T(1,128)} %stack.571) | copy-start | bytes 50692
  119.4 14.6 %copy-start.52 = (f32[2,1,2112]{2,1,0:T(1,128)S(1)}, f32[2,1,2112]{2,1,0:T(1,128)}, u32[]{:S(2)}) copy-start(f32[2,1,2112]{2,1,0:T(1,128)} %stack.572) | copy-start | bytes 50692
  147.5 235.1 %all-gather.2.cloned.1.call-start = ((), (), s32[]{:S(2)}) async-start(), calls=%async_computation.2 | async-start | bytes 1098240 | tf_op jit(solution)/shard_map/all_gather | solution.py:59
  148.3 405.3 %all-reduce.6.cloned.1.call-start = ((), (), s32[]{:S(2)}) async-start(), calls=%async_computation.4 | async-start | bytes 131072
  188.1 10.6 %copy-start.11 = (f32[1,2,1,2080]{3,2,1,0:T(1,128)S(1)}, f32[1,2,1,2080]{3,2,1,0:T(1,128)}, u32[]{:S(2)}) copy-start(f32[1,2,1,2080]{3,2,1,0:T(1,128)} %stack.491) | copy-start | bytes 49924
  188.1 10.6 %copy-start.12 = (f32[1,2,1,2080]{3,2,1,0:T(1,128)S(1)}, f32[1,2,1,2080]{3,2,1,0:T(1,128)}, u32[]{:S(2)}) copy-start(f32[1,2,1,2080]{3,2,1,0:T(1,128)} %stack.508) | copy-start | bytes 49924
  188.1 10.6 %copy-start.13 = (f32[1,2,1,2080]{3,2,1,0:T(1,128)S(1)}, f32[1,2,1,2080]{3,2,1,0:T(1,128)}, u32[]{:S(2)}) copy-start(f32[1,2,1,2080]{3,2,1,0:T(1,128)} %stack.509) | copy-start | bytes 49924
  188.1 10.6 %copy-start.14 = (f32[1,2,1,2080]{3,2,1,0:T(1,128)S(1)}, f32[1,2,1,2080]{3,2,1,0:T(1,128)}, u32[]{:S(2)}) copy-start(f32[1,2,1,2080]{3,2,1,0:T(1,128)} %stack.510) | copy-start | bytes 49924
  188.2 10.6 %copy-start.15 = (f32[1,2,1,2080]{3,2,1,0:T(1,128)S(1)}, f32[1,2,1,2080]{3,2,1,0:T(1,128)}, u32[]{:S(2)}) copy-start(f32[1,2,1,2080]{3,2,1,0:T(1,128)} %stack.511) | copy-start | bytes 49924
  188.2 10.6 %copy-start.16 = (f32[1,2,1,2080]{3,2,1,0:T(1,128)S(1)}, f32[1,2,1,2080]{3,2,1,0:T(1,128)}, u32[]{:S(2)}) copy-start(f32[1,2,1,2080]{3,2,1,0:T(1,128)} %stack.512) | copy-start | bytes 49924
  188.2 10.6 %copy-start.17 = (f32[1,2,1,2080]{3,2,1,0:T(1,128)S(1)}, f32[1,2,1,2080]{3,2,1,0:T(1,128)}, u32[]{:S(2)}) copy-start(f32[1,2,1,2080]{3,2,1,0:T(1,128)} %stack.513) | copy-start | bytes 49924
  188.2 10.6 %copy-start.18 = (f32[1,2,1,2080]{3,2,1,0:T(1,128)S(1)}, f32[1,2,1,2080]{3,2,1,0:T(1,128)}, u32[]{:S(2)}) copy-start(f32[1,2,1,2080]{3,2,1,0:T(1,128)} %stack.514) | copy-start | bytes 49924
  188.2 10.6 %copy-start.19 = (f32[1,2,1,2080]{3,2,1,0:T(1,128)S(1)}, f32[1,2,1,2080]{3,2,1,0:T(1,128)}, u32[]{:S(2)}) copy-start(f32[1,2,1,2080]{3,2,1,0:T(1,128)} %stack.515) | copy-start | bytes 49924
  188.2 10.6 %copy-start.20 = (f32[1,2,1,2080]{3,2,1,0:T(1,128)S(1)}, f32[1,2,1,2080]{3,2,1,0:T(1,128)}, u32[]{:S(2)}) copy-start(f32[1,2,1,2080]{3,2,1,0:T(1,128)} %stack.516) | copy-start | bytes 49924
  188.2 10.6 %copy-start.21 = (f32[1,2,1,2080]{3,2,1,0:T(1,128)S(1)}, f32[1,2,1,2080]{3,2,1,0:T(1,128)}, u32[]{:S(2)}) copy-start(f32[1,2,1,2080]{3,2,1,0:T(1,128)} %stack.517) | copy-start | bytes 49924
  188.2 10.6 %copy-start.22 = (f32[1,2,1,2080]{3,2,1,0:T(1,128)S(1)}, f32[1,2,1,2080]{3,2,1,0:T(1,128)}, u32[]{:S(2)}) copy-start(f32[1,2,1,2080]{3,2,1,0:T(1,128)} %stack.518) | copy-start | bytes 49924
  188.2 10.6 %copy-start.23 = (f32[1,2,1,2080]{3,2,1,0:T(1,128)S(1)}, f32[1,2,1,2080]{3,2,1,0:T(1,128)}, u32[]{:S(2)}) copy-start(f32[1,2,1,2080]{3,2,1,0:T(1,128)} %stack.519) | copy-start | bytes 49924
  188.2 10.6 %copy-start.24 = (f32[1,2,1,2080]{3,2,1,0:T(1,128)S(1)}, f32[1,2,1,2080]{3,2,1,0:T(1,128)}, u32[]{:S(2)}) copy-start(f32[1,2,1,2080]{3,2,1,0:T(1,128)} %stack.520) | copy-start | bytes 49924
  188.3 10.6 %copy-start.25 = (f32[1,2,1,2080]{3,2,1,0:T(1,128)S(1)}, f32[1,2,1,2080]{3,2,1,0:T(1,128)}, u32[]{:S(2)}) copy-start(f32[1,2,1,2080]{3,2,1,0:T(1,128)} %stack.521) | copy-start | bytes 49924
  188.3 10.6 %copy-start.26 = (f32[1,2,1,2080]{3,2,1,0:T(1,128)S(1)}, f32[1,2,1,2080]{3,2,1,0:T(1,128)}, u32[]{:S(2)}) copy-start(f32[1,2,1,2080]{3,2,1,0:T(1,128)} %stack.522) | copy-start | bytes 49924
  188.3 10.6 %copy-start.27 = (f32[1,2,1,2080]{3,2,1,0:T(1,128)S(1)}, f32[1,2,1,2080]{3,2,1,0:T(1,128)}, u32[]{:S(2)}) copy-start(f32[1,2,1,2080]{3,2,1,0:T(1,128)} %stack.523) | copy-start | bytes 49924
  188.3 10.6 %copy-start.28 = (f32[1,2,1,2080]{3,2,1,0:T(1,128)S(1)}, f32[1,2,1,2080]{3,2,1,0:T(1,128)}, u32[]{:S(2)}) copy-start(f32[1,2,1,2080]{3,2,1,0:T(1,128)} %stack.492) | copy-start | bytes 49924
  188.3 10.6 %copy-start.29 = (f32[1,2,1,2080]{3,2,1,0:T(1,128)S(1)}, f32[1,2,1,2080]{3,2,1,0:T(1,128)}, u32[]{:S(2)}) copy-start(f32[1,2,1,2080]{3,2,1,0:T(1,128)} %stack.493) | copy-start | bytes 49924
  188.3 10.6 %copy-start.30 = (f32[1,2,1,2080]{3,2,1,0:T(1,128)S(1)}, f32[1,2,1,2080]{3,2,1,0:T(1,128)}, u32[]{:S(2)}) copy-start(f32[1,2,1,2080]{3,2,1,0:T(1,128)} %stack.494) | copy-start | bytes 49924
  188.3 10.6 %copy-start.31 = (f32[1,2,1,2080]{3,2,1,0:T(1,128)S(1)}, f32[1,2,1,2080]{3,2,1,0:T(1,128)}, u32[]{:S(2)}) copy-start(f32[1,2,1,2080]{3,2,1,0:T(1,128)} %stack.495) | copy-start | bytes 49924
  188.3 10.6 %copy-start.32 = (f32[1,2,1,2080]{3,2,1,0:T(1,128)S(1)}, f32[1,2,1,2080]{3,2,1,0:T(1,128)}, u32[]{:S(2)}) copy-start(f32[1,2,1,2080]{3,2,1,0:T(1,128)} %stack.496) | copy-start | bytes 49924
  188.3 10.6 %copy-start.33 = (f32[1,2,1,2080]{3,2,1,0:T(1,128)S(1)}, f32[1,2,1,2080]{3,2,1,0:T(1,128)}, u32[]{:S(2)}) copy-start(f32[1,2,1,2080]{3,2,1,0:T(1,128)} %stack.497) | copy-start | bytes 49924
  188.3 10.6 %copy-start.34 = (f32[1,2,1,2080]{3,2,1,0:T(1,128)S(1)}, f32[1,2,1,2080]{3,2,1,0:T(1,128)}, u32[]{:S(2)}) copy-start(f32[1,2,1,2080]{3,2,1,0:T(1,128)} %stack.498) | copy-start | bytes 49924
  188.4 10.6 %copy-start.35 = (f32[1,2,1,2080]{3,2,1,0:T(1,128)S(1)}, f32[1,2,1,2080]{3,2,1,0:T(1,128)}, u32[]{:S(2)}) copy-start(f32[1,2,1,2080]{3,2,1,0:T(1,128)} %stack.499) | copy-start | bytes 49924
  188.4 10.6 %copy-start.36 = (f32[1,2,1,2080]{3,2,1,0:T(1,128)S(1)}, f32[1,2,1,2080]{3,2,1,0:T(1,128)}, u32[]{:S(2)}) copy-start(f32[1,2,1,2080]{3,2,1,0:T(1,128)} %stack.500) | copy-start | bytes 49924
  194.6 10.0 %copy-start.41 = (f32[1,2,1,2080]{3,2,1,0:T(1,128)S(1)}, f32[1,2,1,2080]{3,2,1,0:T(1,128)}, u32[]{:S(2)}) copy-start(f32[1,2,1,2080]{3,2,1,0:T(1,128)} %stack.545) | copy-start | bytes 49924
  194.6 10.0 %copy-start.42 = (f32[1,2,1,2080]{3,2,1,0:T(1,128)S(1)}, f32[1,2,1,2080]{3,2,1,0:T(1,128)}, u32[]{:S(2)}) copy-start(f32[1,2,1,2080]{3,2,1,0:T(1,128)} %stack.546) | copy-start | bytes 49924
  194.6 10.0 %copy-start.43 = (f32[1,2,1,2080]{3,2,1,0:T(1,128)S(1)}, f32[1,2,1,2080]{3,2,1,0:T(1,128)}, u32[]{:S(2)}) copy-start(f32[1,2,1,2080]{3,2,1,0:T(1,128)} %stack.547) | copy-start | bytes 49924
  194.6 10.0 %copy-start.44 = (f32[1,2,1,2080]{3,2,1,0:T(1,128)S(1)}, f32[1,2,1,2080]{3,2,1,0:T(1,128)}, u32[]{:S(2)}) copy-start(f32[1,2,1,2080]{3,2,1,0:T(1,128)} %stack.548) | copy-start | bytes 49924
  194.6 10.0 %copy-start.45 = (f32[1,2,1,2080]{3,2,1,0:T(1,128)S(1)}, f32[1,2,1,2080]{3,2,1,0:T(1,128)}, u32[]{:S(2)}) copy-start(f32[1,2,1,2080]{3,2,1,0:T(1,128)} %stack.549) | copy-start | bytes 49924
  397.8 169.1 %copy-start.54 = (s32[16]{0:T(128)S(1)}, s32[16]{0:T(128)}, u32[]{:S(2)}) copy-start(s32[16]{0:T(128)} %copy-done.53) | copy-start | bytes 196
  555.1 20.7 %all-to-all-start.1 = ((f32[2,1,2,128]{0,2,1,3:T(2,128)}), f32[2,1,2,128]{0,2,1,3:T(2,128)S(1)}, u32[]{:S(2)}, u32[]{:S(2)}) async-start(f32[2,1,2,128]{0,2,1,3:T(2,128)} %copy.577), calls=%async_computation.1 | async-start | bytes 262144 | tf_op jit(solution)/shard_map/all_to_all | solution.py:132
  (14 other events, 99.3 us)
Sparse Core Ops, SparseCore 0:
  147.6 152.2 all-reduce.3
  303.1 79.4 all-gather.1
  402.2 151.3 all-reduce.5
where the time goes:
time: 587 us; the launch traced here: 583 us
  waiting for transfers between devices  313 us (53%)
  local copies, waits for them, and re-layouts  147 us (25%)
  blocking collectives  41.2 us (7%)
  other arithmetic  27.8 us (5%)
  starting transfers between devices  22.2 us (4%)
  matrix products  18.2 us (3%)
  between operations  14.9 us (3%)
    unnamed x4, waiting for transfers between devices  150 us
    psum x1, waiting for transfers between devices, body(): lax.psum(jnp.einsum('afbp,afbq->fpq', own_sketch, own_sketch, precision=h...  89 us
    all_gather x1, waiting for transfers between devices, body(): sketch = lax.all_gather(own_sketch, 'trace', axis=0, tiled=True)  58.3 us
    another operation x66, local copies, waits for them, and re-layouts, body(): jnp.stack([row_slabs[..., anchor:anchor + lag_y] for anchor in range(win_...  53 us
    another operation x68, local copies, waits for them, and re-layouts, body(): jnp.stack([band[:, :, anchor:anchor + win_x] for anchor in range(lag_x)],...  51 us
    all_gather x1, blocking collectives, body(): whole_slices = lax.all_gather(slices, 'trace', axis=2, tiled=True)  41.2 us
    slice x69, local copies, waits for them, and re-layouts, body(): row_slabs[..., anchor:anchor + lag_y]  21.6 us
    another operation x3, other arithmetic, body(): factor = jnp.linalg.cholesky(real_gram)  12.6 us
  transfers between devices with their start and end apart: 5, of which 5 were waited for; matrix products, arithmetic and copies ran while one was open for 15% of the time, Pallas kernels for 0%

commit v1 on v0

--- a/solution.py
+++ b/solution.py
@@ -44,7 +44,8 @@
     spectrum = jnp.einsum("xyt,tpk->xypk", traces.astype(jnp.float32), forward, precision=highest)
     spectrum = lax.all_to_all(spectrum, "freq", split_axis=3, concat_axis=1, tiled=True)
     slices = jnp.transpose(spectrum, (3, 2, 0, 1))
-    whole_slices = lax.all_gather(slices, "trace", axis=2, tiled=True)
+    copies = jnp.concatenate([slices] * lax.axis_size("trace"), axis=2)
+    whole_slices = lax.all_to_all(copies, "trace", 2, 2, tiled=True)
     freq_dev = whole_slices.shape[0]
     first_row = position * own_rows
     row_slabs = jnp.stack([lax.dynamic_slice_in_dim(whole_slices, first_row + 0, lag_x, 2)], axis=1)

time: 587 us -> 571 us (0.973)
  blocking collectives: 41.2 us -> 16.7 us
  local copies, waits for them, and re-layouts: 147 us -> 164 us
  waiting for transfers between devices: 313 us -> 301 us
    all_gather x1 -> x0, blocking collectives: 41.2 us -> none  [body(): whole_slices = lax.all_gather(slices, 'trace', axis=2, tiled=True)]
    unnamed x115 -> x146, local copies, waits for them, and re-layouts: 2.14 us -> 20.1 us
    all_to_all x0 -> x1, blocking collectives: none -> 16.7 us  [body(): lax.all_to_all(spectrum, 'freq', split_axis=3, concat_axis=1, tiled=True)]
    psum x1, waiting for transfers between devices: 89 us -> 76.2 us  [body(): lax.psum(jnp.einsum('afbp,afbq->fpq', own_sketch, own_sketch, precision=h...]
  transfers between devices with their start and end apart: 5 -> 5, of which waited for: 5 -> 5; matrix products, arithmetic and copies ran while one was open for 15% -> 16% of each run, Pallas kernels for 0% -> 0%
where the time goes in v1:
time: 571 us; the launch traced here: 567 us
  waiting for transfers between devices  301 us (53%)
  local copies, waits for them, and re-layouts  164 us (29%)
  other arithmetic  27.8 us (5%)
  starting transfers between devices  24 us (4%)
  matrix products  18.2 us (3%)
  blocking collectives  16.7 us (3%)
  between operations  14.9 us (3%)
    unnamed x4, waiting for transfers between devices  150 us
    psum x1, waiting for transfers between devices, body(): lax.psum(jnp.einsum('afbp,afbq->fpq', own_sketch, own_sketch, precision=h...  76.2 us
    all_gather x1, waiting for transfers between devices, body(): sketch = lax.all_gather(own_sketch, 'trace', axis=0, tiled=True)  58.3 us
    another operation x66, local copies, waits for them, and re-layouts, body(): jnp.stack([row_slabs[..., anchor:anchor + lag_y] for anchor in range(win_...  53 us
    another operation x68, local copies, waits for them, and re-layouts, body(): jnp.stack([band[:, :, anchor:anchor + win_x] for anchor in range(lag_x)],...  51 us
    slice x69, local copies, waits for them, and re-layouts, body(): row_slabs[..., anchor:anchor + lag_y]  21.6 us
    unnamed x146, local copies, waits for them, and re-layouts  20.1 us
    all_to_all x1, blocking collectives, body(): lax.all_to_all(spectrum, 'freq', split_axis=3, concat_axis=1, tiled=True)  16.7 us
  transfers between devices with their start and end apart: 5, of which 5 were waited for; matrix products, arithmetic and copies ran while one was open for 16% of the time, Pallas kernels for 0%

profile of v1, /device:TPU:1, one launch (start us, length us, event | category | flops | bytes accessed | tf_op | source)
XLA Modules:
  0.0 567.3 jit_solution(12122509520955512131)
XLA Ops:
  7.2 1.4 convolution_bitcast_fusion.5
  8.7 16.7 %all_to_all.41 = f32[2,8,2,16]{1,0,2,3:T(2,128)S(1)} all-to-all(f32[2,8,2,16]{1,0,2,3:T(2,128)S(1)} %copy.367), channel_id=1, replica_groups=mesh['freq'=16,'trace'=32] {'freq'}, dimensions={3} | all-to-all | bytes 4096 | tf_op jit(solution)/shard_map/all_to_all | solution.py:45
  44.0 12.0 %all-to-all-start.1 = ((f32[1,2,64,128]{3,1,0,2:T(2,128)}), f32[1,2,64,128]{3,1,0,2:T(2,128)S(1)}, u32[]{:S(2)}, u32[]{:S(2)}) async-start(f32[1,2,64,128]{3,1,0,2:T(2,128)} %bitcast.7), calls=%async_computation.1 | async-start | bytes 131072 | tf_op jit(solution)/shard_map/all_to_all | solution.py:48
  56.1 8.8 %all-to-all-done.1 = f32[1,2,64,128]{3,1,0,2:T(2,128)S(1)} async-done(((f32[1,2,64,128]{3,1,0,2:T(2,128)}), f32[1,2,64,128]{3,1,0,2:T(2,128)S(1)}, u32[]{:S(2)}, u32[]{:S(2)}) %all-to-all-start.1) | async-done | bytes 65568 | tf_op jit(solution)/shard_map/all_to_all | solution.py:48
  64.8 1.5 fusion.69
  66.4 1.4 fusion.68
  68.5 1.0 fusion.70
  69.6 0.8 copy.379
  71.0 0.8 copy.380
  72.4 0.8 copy.381
  73.9 0.8 copy.382
  75.3 0.8 copy.383
  76.8 0.8 copy.384
  78.2 0.8 copy.385
  79.7 0.8 copy.386
  81.1 0.8 copy.387
  82.6 0.8 copy.388
  84.0 0.8 copy.389
  85.5 0.8 copy.390
  86.9 0.8 copy.391
  88.4 0.8 copy.392
  89.8 0.8 copy.393
  91.3 0.8 copy.394
  92.8 0.8 copy.395
  98.5 0.8 copy.399
  100.0 0.8 copy.400
  130.5 9.0 %stack.490 = f32[2,65,2112]{2,1,0:T(8,128)S(1)} concatenate(f32[2,1,2112]{2,1,0:T(1,128)} %stack.562, f32[2,1,2112]{2,1,0:T(1,128)} %stack.563, f32[2,1,2112]{2,1,0:T(1,128)} %stack.564, f32[2,1,2112]{2,1,0:T(1,128)} %stack.565, f32[2,1,2112]{2,1,0:T(1,128)} %stack.566, f32[2,1,2112]{2,1,0:T(1,128)} %stack.567, f32[2,1,2112]{2,1,0:T(1,128)} %stack.568, f32[2,1,2112]{2,1,0:T(1,128)} %stack.569, ...), dimensions={1} | concatenate | bytes 2196480 | tf_op jit(solution)/shard_map/stack | solution.py:52
  139.5 3.6 fusion.6
  143.2 0.9 convolution_bitcast_fusion.3
  146.4 1.2 constant_dynamic-slice_fusion.65
  159.9 1.8 constant_dynamic-slice_fusion.47
  195.6 5.6 stack.524
  201.2 6.3 %stack.558 = f32[1,2,33,2080]{3,2,1,0:T(8,128)} concatenate(f32[1,2,1,2080]{3,2,1,0:T(1,128)S(1)} %copy-done.37, f32[1,2,1,2080]{3,2,1,0:T(1,128)} %stack.526, f32[1,2,1,2080]{3,2,1,0:T(1,128)} %stack.527, f32[1,2,1,2080]{3,2,1,0:T(1,128)} %stack.528, f32[1,2,1,2080]{3,2,1,0:T(1,128)S(1)} %copy-done.48, f32[1,2,1,2080]{3,2,1,0:T(1,128)S(1)} %copy-done.49, ...), dimensions={2} | concatenate | bytes 1098240 | tf_op jit(solution)/shard_map/stack | solution.py:69
  207.6 76.2 %all-reduce.4.cloned.1.call-done = f32[1,128,128]{1,2,0:T(8,128)} async-done(((f32[1,128,128]{1,2,0:T(8,128)}), f32[1,128,128]{1,2,0:T(8,128)}) %all-reduce.4.cloned.1.call-update) | async-done | bytes 65552 | tf_op jit(solution)/shard_map/psum | solution.py:61
  283.8 0.9 fusion.66
  285.0 11.9 %custom-call.11 = f32[1,128,128]{2,1,0:T(8,128)S(1)} custom-call(f32[1,128,128]{2,1,0:T(8,128)S(1)} %fusion.46), custom_call_target="Cholesky" | custom-call | tf_op jit(solution)/shard_map/jit(cholesky)/cholesky | solution.py:94
  298.3 9.8 %custom-call.12 = f32[1,1,128,128]{2,3,1,0:T(8,128)S(1)} custom-call(f32[1,1,128,128]{3,2,1,0:T(8,128)S(1)} %fusion.41), custom_call_target="InvertDiagBlocksLowerTriangular" | custom-call | tf_op jit(solution)/shard_map/vmap(jit(_cho_solve))/triangular_solve | solution.py:25
  308.1 58.3 %all-gather.2.cloned.1.call-done = f32[32,1,65,128]{3,1,2,0:T(1,128)} async-done(((f32[1,1,65,128]{3,1,2,0:T(1,128)}), f32[32,1,65,128]{3,1,2,0:T(1,128)}) %all-gather.2.cloned.1.call-update) | async-done | bytes 1064976 | tf_op jit(solution)/shard_map/all_gather | solution.py:60
  366.4 3.1 fusion.9
  370.5 5.1 convolution_bitcast_fusion.1
  375.6 6.0 %copy.575 = f32[1,65,2,2,33,32]{1,5,4,3,2,0:T(8,128)} copy(f32[1,65,2,2,33,32]{4,5,3,2,1,0:T(8,128)} %convolution_bitcast_fusion.1) | data formatting | bytes 2196480 | tf_op jit(solution)/shard_map/fqezc,fbqa->fbezca/transpose | solution.py:106
  381.6 2.6 convolution_bitcast_fusion.2
  386.0 1.3 dynamic-slice.1
  388.0 149.5 %all-reduce.6.cloned.1.call-done = f32[64,1,2,128]{3,0,2,1:T(8,128)} async-done(((f32[64,1,2,128]{3,0,2,1:T(8,128)}), f32[64,1,2,128]{3,0,2,1:T(8,128)}) %all-reduce.6.cloned.1.call-update) | async-done | bytes 65552
  538.1 0.8 copy.577
  538.9 11.8 %all-to-all-start.2 = ((f32[2,1,2,128]{0,2,1,3:T(2,128)}), f32[2,1,2,128]{0,2,1,3:T(2,128)S(1)}, u32[]{:S(2)}, u32[]{:S(2)}) async-start(f32[2,1,2,128]{0,2,1,3:T(2,128)} %copy.577), calls=%async_computation.2 | async-start | bytes 262144 | tf_op jit(solution)/shard_map/all_to_all | solution.py:133
  551.3 8.3 %all-to-all-done.2 = f32[2,1,2,128]{0,2,1,3:T(2,128)S(1)} async-done(((f32[2,1,2,128]{0,2,1,3:T(2,128)}), f32[2,1,2,128]{0,2,1,3:T(2,128)S(1)}, u32[]{:S(2)}, u32[]{:S(2)}) %all-to-all-start.2) | async-done | bytes 2080 | tf_op jit(solution)/shard_map/all_to_all | solution.py:133
  559.8 1.0 convolution_bitcast_fusion
  (434 shorter events, 120.1 us)
Async XLA Ops:
  6.5 133.0 %copy-start = (f32[2,33,64,64]{3,2,1,0:T(8,128)S(1)}, f32[2,33,64,64]{3,2,1,0:T(8,128)}, u32[]{:S(2)}) copy-start(f32[2,33,64,64]{3,2,1,0:T(8,128)} %param.3) | copy-start | bytes 3244036
  44.0 20.8 %all-to-all-start.1 = ((f32[1,2,64,128]{3,1,0,2:T(2,128)}), f32[1,2,64,128]{3,1,0,2:T(2,128)S(1)}, u32[]{:S(2)}, u32[]{:S(2)}) async-start(f32[1,2,64,128]{3,1,0,2:T(2,128)} %bitcast.7), calls=%async_computation.1 | async-start | bytes 131072 | tf_op jit(solution)/shard_map/all_to_all | solution.py:48
  56.0 227.8 %all-reduce.4.cloned.1.call-start = ((), (), s32[]{:S(2)}) async-start(), calls=%async_computation.4 | async-start | bytes 131072 | tf_op jit(solution)/shard_map/psum | solution.py:61
  110.4 14.5 %copy-start.10 = (f32[1,1,2,33,64]{4,2,3,1,0:T(2,128)S(1)}, f32[1,1,2,33,64]{4,2,3,1,0:T(2,128)}, u32[]{:S(2)}) copy-start(f32[1,1,2,33,64]{4,2,3,1,0:T(2,128)} %get-tuple-element.145) | copy-start | bytes 50692
  111.1 14.5 %copy-start.9 = (f32[1,1,2,33,64]{4,2,3,1,0:T(2,128)S(1)}, f32[1,1,2,33,64]{4,2,3,1,0:T(2,128)}, u32[]{:S(2)}) copy-start(f32[1,1,2,33,64]{4,2,3,1,0:T(2,128)} %get-tuple-element.144) | copy-start | bytes 50692
  111.8 14.6 %copy-start.8 = (f32[1,1,2,33,64]{4,2,3,1,0:T(2,128)S(1)}, f32[1,1,2,33,64]{4,2,3,1,0:T(2,128)}, u32[]{:S(2)}) copy-start(f32[1,1,2,33,64]{4,2,3,1,0:T(2,128)} %get-tuple-element.143) | copy-start | bytes 50692
  112.5 14.5 %copy-start.7 = (f32[1,1,2,33,64]{4,2,3,1,0:T(2,128)S(1)}, f32[1,1,2,33,64]{4,2,3,1,0:T(2,128)}, u32[]{:S(2)}) copy-start(f32[1,1,2,33,64]{4,2,3,1,0:T(2,128)} %get-tuple-element.142) | copy-start | bytes 50692
  113.2 14.5 %copy-start.6 = (f32[1,1,2,33,64]{4,2,3,1,0:T(2,128)S(1)}, f32[1,1,2,33,64]{4,2,3,1,0:T(2,128)}, u32[]{:S(2)}) copy-start(f32[1,1,2,33,64]{4,2,3,1,0:T(2,128)} %get-tuple-element.141) | copy-start | bytes 50692
  113.9 14.5 %copy-start.5 = (f32[1,1,2,33,64]{4,2,3,1,0:T(2,128)S(1)}, f32[1,1,2,33,64]{4,2,3,1,0:T(2,128)}, u32[]{:S(2)}) copy-start(f32[1,1,2,33,64]{4,2,3,1,0:T(2,128)} %get-tuple-element.140) | copy-start | bytes 50692
  114.6 14.6 %copy-start.4 = (f32[1,1,2,33,64]{4,2,3,1,0:T(2,128)S(1)}, f32[1,1,2,33,64]{4,2,3,1,0:T(2,128)}, u32[]{:S(2)}) copy-start(f32[1,1,2,33,64]{4,2,3,1,0:T(2,128)} %get-tuple-element.139) | copy-start | bytes 50692
  115.3 14.5 %copy-start.3 = (f32[1,1,2,33,64]{4,2,3,1,0:T(2,128)S(1)}, f32[1,1,2,33,64]{4,2,3,1,0:T(2,128)}, u32[]{:S(2)}) copy-start(f32[1,1,2,33,64]{4,2,3,1,0:T(2,128)} %get-tuple-element.138) | copy-start | bytes 50692
  116.0 14.6 %copy-start.51 = (f32[2,1,2112]{2,1,0:T(1,128)S(1)}, f32[2,1,2112]{2,1,0:T(1,128)}, u32[]{:S(2)}) copy-start(f32[2,1,2112]{2,1,0:T(1,128)} %stack.571) | copy-start | bytes 50692
  116.0 14.6 %copy-start.52 = (f32[2,1,2112]{2,1,0:T(1,128)S(1)}, f32[2,1,2112]{2,1,0:T(1,128)}, u32[]{:S(2)}) copy-start(f32[2,1,2112]{2,1,0:T(1,128)} %stack.572) | copy-start | bytes 50692
  144.1 222.4 %all-gather.2.cloned.1.call-start = ((), (), s32[]{:S(2)}) async-start(), calls=%async_computation.3 | async-start | bytes 1098240 | tf_op jit(solution)/shard_map/all_gather | solution.py:60
  144.9 392.5 %all-reduce.6.cloned.1.call-start = ((), (), s32[]{:S(2)}) async-start(), calls=%async_computation.5 | async-start | bytes 131072
  184.7 10.6 %copy-start.11 = (f32[1,2,1,2080]{3,2,1,0:T(1,128)S(1)}, f32[1,2,1,2080]{3,2,1,0:T(1,128)}, u32[]{:S(2)}) copy-start(f32[1,2,1,2080]{3,2,1,0:T(1,128)} %stack.491) | copy-start | bytes 49924
  184.7 10.6 %copy-start.12 = (f32[1,2,1,2080]{3,2,1,0:T(1,128)S(1)}, f32[1,2,1,2080]{3,2,1,0:T(1,128)}, u32[]{:S(2)}) copy-start(f32[1,2,1,2080]{3,2,1,0:T(1,128)} %stack.508) | copy-start | bytes 49924
  184.7 10.6 %copy-start.13 = (f32[1,2,1,2080]{3,2,1,0:T(1,128)S(1)}, f32[1,2,1,2080]{3,2,1,0:T(1,128)}, u32[]{:S(2)}) copy-start(f32[1,2,1,2080]{3,2,1,0:T(1,128)} %stack.509) | copy-start | bytes 49924
  184.7 10.6 %copy-start.14 = (f32[1,2,1,2080]{3,2,1,0:T(1,128)S(1)}, f32[1,2,1,2080]{3,2,1,0:T(1,128)}, u32[]{:S(2)}) copy-start(f32[1,2,1,2080]{3,2,1,0:T(1,128)} %stack.510) | copy-start | bytes 49924
  184.7 10.6 %copy-start.15 = (f32[1,2,1,2080]{3,2,1,0:T(1,128)S(1)}, f32[1,2,1,2080]{3,2,1,0:T(1,128)}, u32[]{:S(2)}) copy-start(f32[1,2,1,2080]{3,2,1,0:T(1,128)} %stack.511) | copy-start | bytes 49924
  184.8 10.6 %copy-start.16 = (f32[1,2,1,2080]{3,2,1,0:T(1,128)S(1)}, f32[1,2,1,2080]{3,2,1,0:T(1,128)}, u32[]{:S(2)}) copy-start(f32[1,2,1,2080]{3,2,1,0:T(1,128)} %stack.512) | copy-start | bytes 49924
  184.8 10.6 %copy-start.17 = (f32[1,2,1,2080]{3,2,1,0:T(1,128)S(1)}, f32[1,2,1,2080]{3,2,1,0:T(1,128)}, u32[]{:S(2)}) copy-start(f32[1,2,1,2080]{3,2,1,0:T(1,128)} %stack.513) | copy-start | bytes 49924
  184.8 10.6 %copy-start.18 = (f32[1,2,1,2080]{3,2,1,0:T(1,128)S(1)}, f32[1,2,1,2080]{3,2,1,0:T(1,128)}, u32[]{:S(2)}) copy-start(f32[1,2,1,2080]{3,2,1,0:T(1,128)} %stack.514) | copy-start | bytes 49924
  184.8 10.6 %copy-start.19 = (f32[1,2,1,2080]{3,2,1,0:T(1,128)S(1)}, f32[1,2,1,2080]{3,2,1,0:T(1,128)}, u32[]{:S(2)}) copy-start(f32[1,2,1,2080]{3,2,1,0:T(1,128)} %stack.515) | copy-start | bytes 49924
  184.8 10.6 %copy-start.20 = (f32[1,2,1,2080]{3,2,1,0:T(1,128)S(1)}, f32[1,2,1,2080]{3,2,1,0:T(1,128)}, u32[]{:S(2)}) copy-start(f32[1,2,1,2080]{3,2,1,0:T(1,128)} %stack.516) | copy-start | bytes 49924
  184.8 10.6 %copy-start.21 = (f32[1,2,1,2080]{3,2,1,0:T(1,128)S(1)}, f32[1,2,1,2080]{3,2,1,0:T(1,128)}, u32[]{:S(2)}) copy-start(f32[1,2,1,2080]{3,2,1,0:T(1,128)} %stack.517) | copy-start | bytes 49924
  184.8 10.6 %copy-start.22 = (f32[1,2,1,2080]{3,2,1,0:T(1,128)S(1)}, f32[1,2,1,2080]{3,2,1,0:T(1,128)}, u32[]{:S(2)}) copy-start(f32[1,2,1,2080]{3,2,1,0:T(1,128)} %stack.518) | copy-start | bytes 49924
  184.8 10.6 %copy-start.23 = (f32[1,2,1,2080]{3,2,1,0:T(1,128)S(1)}, f32[1,2,1,2080]{3,2,1,0:T(1,128)}, u32[]{:S(2)}) copy-start(f32[1,2,1,2080]{3,2,1,0:T(1,128)} %stack.519) | copy-start | bytes 49924
  184.8 10.6 %copy-start.24 = (f32[1,2,1,2080]{3,2,1,0:T(1,128)S(1)}, f32[1,2,1,2080]{3,2,1,0:T(1,128)}, u32[]{:S(2)}) copy-start(f32[1,2,1,2080]{3,2,1,0:T(1,128)} %stack.520) | copy-start | bytes 49924
  184.8 10.6 %copy-start.25 = (f32[1,2,1,2080]{3,2,1,0:T(1,128)S(1)}, f32[1,2,1,2080]{3,2,1,0:T(1,128)}, u32[]{:S(2)}) copy-start(f32[1,2,1,2080]{3,2,1,0:T(1,128)} %stack.521) | copy-start | bytes 49924
  184.9 10.6 %copy-start.26 = (f32[1,2,1,2080]{3,2,1,0:T(1,128)S(1)}, f32[1,2,1,2080]{3,2,1,0:T(1,128)}, u32[]{:S(2)}) copy-start(f32[1,2,1,2080]{3,2,1,0:T(1,128)} %stack.522) | copy-start | bytes 49924
  184.9 10.6 %copy-start.27 = (f32[1,2,1,2080]{3,2,1,0:T(1,128)S(1)}, f32[1,2,1,2080]{3,2,1,0:T(1,128)}, u32[]{:S(2)}) copy-start(f32[1,2,1,2080]{3,2,1,0:T(1,128)} %stack.523) | copy-start | bytes 49924
  184.9 10.6 %copy-start.28 = (f32[1,2,1,2080]{3,2,1,0:T(1,128)S(1)}, f32[1,2,1,2080]{3,2,1,0:T(1,128)}, u32[]{:S(2)}) copy-start(f32[1,2,1,2080]{3,2,1,0:T(1,128)} %stack.492) | copy-start | bytes 49924
  184.9 10.6 %copy-start.29 = (f32[1,2,1,2080]{3,2,1,0:T(1,128)S(1)}, f32[1,2,1,2080]{3,2,1,0:T(1,128)}, u32[]{:S(2)}) copy-start(f32[1,2,1,2080]{3,2,1,0:T(1,128)} %stack.493) | copy-start | bytes 49924
  184.9 10.6 %copy-start.30 = (f32[1,2,1,2080]{3,2,1,0:T(1,128)S(1)}, f32[1,2,1,2080]{3,2,1,0:T(1,128)}, u32[]{:S(2)}) copy-start(f32[1,2,1,2080]{3,2,1,0:T(1,128)} %stack.494) | copy-start | bytes 49924
  184.9 10.6 %copy-start.31 = (f32[1,2,1,2080]{3,2,1,0:T(1,128)S(1)}, f32[1,2,1,2080]{3,2,1,0:T(1,128)}, u32[]{:S(2)}) copy-start(f32[1,2,1,2080]{3,2,1,0:T(1,128)} %stack.495) | copy-start | bytes 49924
  184.9 10.6 %copy-start.32 = (f32[1,2,1,2080]{3,2,1,0:T(1,128)S(1)}, f32[1,2,1,2080]{3,2,1,0:T(1,128)}, u32[]{:S(2)}) copy-start(f32[1,2,1,2080]{3,2,1,0:T(1,128)} %stack.496) | copy-start | bytes 49924
  184.9 10.6 %copy-start.33 = (f32[1,2,1,2080]{3,2,1,0:T(1,128)S(1)}, f32[1,2,1,2080]{3,2,1,0:T(1,128)}, u32[]{:S(2)}) copy-start(f32[1,2,1,2080]{3,2,1,0:T(1,128)} %stack.497) | copy-start | bytes 49924
  184.9 10.6 %copy-start.34 = (f32[1,2,1,2080]{3,2,1,0:T(1,128)S(1)}, f32[1,2,1,2080]{3,2,1,0:T(1,128)}, u32[]{:S(2)}) copy-start(f32[1,2,1,2080]{3,2,1,0:T(1,128)} %stack.498) | copy-start | bytes 49924
  184.9 10.6 %copy-start.35 = (f32[1,2,1,2080]{3,2,1,0:T(1,128)S(1)}, f32[1,2,1,2080]{3,2,1,0:T(1,128)}, u32[]{:S(2)}) copy-start(f32[1,2,1,2080]{3,2,1,0:T(1,128)} %stack.499) | copy-start | bytes 49924
  185.0 10.6 %copy-start.36 = (f32[1,2,1,2080]{3,2,1,0:T(1,128)S(1)}, f32[1,2,1,2080]{3,2,1,0:T(1,128)}, u32[]{:S(2)}) copy-start(f32[1,2,1,2080]{3,2,1,0:T(1,128)} %stack.500) | copy-start | bytes 49924
  191.2 10.0 %copy-start.41 = (f32[1,2,1,2080]{3,2,1,0:T(1,128)S(1)}, f32[1,2,1,2080]{3,2,1,0:T(1,128)}, u32[]{:S(2)}) copy-start(f32[1,2,1,2080]{3,2,1,0:T(1,128)} %stack.545) | copy-start | bytes 49924
  191.2 10.0 %copy-start.42 = (f32[1,2,1,2080]{3,2,1,0:T(1,128)S(1)}, f32[1,2,1,2080]{3,2,1,0:T(1,128)}, u32[]{:S(2)}) copy-start(f32[1,2,1,2080]{3,2,1,0:T(1,128)} %stack.546) | copy-start | bytes 49924
  191.2 10.0 %copy-start.43 = (f32[1,2,1,2080]{3,2,1,0:T(1,128)S(1)}, f32[1,2,1,2080]{3,2,1,0:T(1,128)}, u32[]{:S(2)}) copy-start(f32[1,2,1,2080]{3,2,1,0:T(1,128)} %stack.547) | copy-start | bytes 49924
  191.2 10.0 %copy-start.44 = (f32[1,2,1,2080]{3,2,1,0:T(1,128)S(1)}, f32[1,2,1,2080]{3,2,1,0:T(1,128)}, u32[]{:S(2)}) copy-start(f32[1,2,1,2080]{3,2,1,0:T(1,128)} %stack.548) | copy-start | bytes 49924
  191.2 10.0 %copy-start.45 = (f32[1,2,1,2080]{3,2,1,0:T(1,128)S(1)}, f32[1,2,1,2080]{3,2,1,0:T(1,128)}, u32[]{:S(2)}) copy-start(f32[1,2,1,2080]{3,2,1,0:T(1,128)} %stack.549) | copy-start | bytes 49924
  381.6 169.1 %copy-start.54 = (s32[16]{0:T(128)S(1)}, s32[16]{0:T(128)}, u32[]{:S(2)}) copy-start(s32[16]{0:T(128)} %copy-done.53) | copy-start | bytes 196
  538.9 20.7 %all-to-all-start.2 = ((f32[2,1,2,128]{0,2,1,3:T(2,128)}), f32[2,1,2,128]{0,2,1,3:T(2,128)S(1)}, u32[]{:S(2)}, u32[]{:S(2)}) async-start(f32[2,1,2,128]{0,2,1,3:T(2,128)} %copy.577), calls=%async_computation.2 | async-start | bytes 262144 | tf_op jit(solution)/shard_map/all_to_all | solution.py:133
  (14 other events, 99.3 us)
Sparse Core Ops, SparseCore 0:
  144.2 139.5 all-reduce.3
  287.0 79.4 all-gather.1
  386.1 151.3 all-reduce.5
